TPU v7x, 256 devices: a whole 4x4x8 slice. The times are simulated.
256 devices in a mesh: tile: 16 (over z, core), tensor: 16 (over y, x).
Axes of the slice: x: 4, y: 4, z: 8, core: 2. Of those that a mesh axis runs over, the one named last changes fastest.
Arguments:
- image_hidden: bfloat16 [8, 32, 32, 3072], P(None, 'tile', 'tensor'), may hold values from -6 to 6
- text_hidden: bfloat16 [8, 512, 3072], P(None, ('tile', 'tensor')), may hold values from -6 to 6
- latents: float32 [8, 32, 2048], P(None, 'tile', 'tensor'), may hold values from -6 to 6
- step_index: int32 [8], replicated, may hold values from 0 to 27
- anchor: int32 [8, 2], replicated, may hold values from 0 to 63
- text_len: int32 [8], replicated, may hold values from 64 to 512
- mod_image: float32 [8, 3, 3072], replicated, may hold values from -3 to 3
- mod_text: float32 [8, 3, 3072], replicated, may hold values from -3 to 3
- mod_mlp: float32 [8, 3, 3072], replicated, may hold values from -3 to 3
- mod_final: float32 [8, 2, 3072], replicated, may hold values from -3 to 3
- qkv_image: bfloat16 [3072, 3, 2048], P(None, None, 'tensor'), may hold values from -0.109375 to 0.109375
- qkv_text: bfloat16 [3072, 3, 2048], P(None, None, 'tensor'), may hold values from -0.109375 to 0.109375
- proj_image: bfloat16 [2048, 3072], P('tensor'), may hold values from -0.125 to 0.125
- proj_text: bfloat16 [2048, 3072], P('tensor'), may hold values from -0.125 to 0.125
- qk_gain: float32 [2, 2, 128], replicated, may hold values from 0.5 to 10
- mlp_expand: bfloat16 [3072, 6144], P(None, 'tensor'), may hold values from -0.109375 to 0.109375
- mlp_reduce: bfloat16 [6144, 3072], P('tensor'), may hold values from -0.078125 to 0.078125
- final_weight: bfloat16 [3072, 64], replicated, may hold values from -0.109375 to 0.109375
Outputs:
- image_out: bfloat16 [8, 32, 32, 3072], P(None, 'tile', 'tensor')
- text_out: bfloat16 [8, 512, 3072], P(None, ('tile', 'tensor'))
- latents_ext: float32 [8, 64, 2048], P(None, 'tile', 'tensor')
Inputs may be any that keep to these rules, and one draw needn't show every extreme that they name: text_len gives each request's live text tokens; slots at or past it take no part as keys. step_index is a step of the 28-step plan.
All inputs are finite; a program needn't handle non-finite values.
Results may differ from a plain program's by a relative error of at most 0.0085.
The roundings to bfloat16 on the way count: a program that leaves them out, or rounds other values in their place, can miss the bound.
Values may be sent and summed in bfloat16 or wider, within the bound.
No kernel may reach another device: no remote copies, remote signals or barrier semaphores. Data moves between devices by JAX's collectives and lax.ppermute only.
A program may use at most 128 MiB of HBM per device.

v0:
```python
import math
import jax
import jax.numpy as jnp
from jax import lax
from jax.sharding import PartitionSpec as P

HEAD_DIM = 128
GRID = 32
NSTEPS = 28
norm_eps = 1e-06
time_shift = 3.0


def padded(value, sides, width):
    for axis, dim in sides:
        size, length = (lax.axis_size(axis), value.shape[dim])
        up = [(i, (i + 1) % size) for i in range(size - 1)]
        down = [(j, i) for i, j in up]
        last = lax.slice_in_dim(value, length - width, length, axis=dim)
        leading = lax.slice_in_dim(value, 0, width, axis=dim)
        before = lax.ppermute(last, axis, up)
        after = lax.ppermute(leading, axis, down)
        value = jnp.concatenate([before, value, after], axis=dim)
    return value


def layer_norm(values):
    average = jnp.mean(values, -1, keepdims=True)
    centred = values - average
    spread = jnp.mean(centred * centred, -1, keepdims=True)
    return centred * lax.rsqrt(spread + norm_eps)


def modulate(hidden, shift, stretch):
    normed = layer_norm(hidden.astype(jnp.float32))
    return ((1.0 + stretch) * normed + shift).astype(jnp.bfloat16)


def rope_tables(row_ids, col_ids):
    pair_index = jnp.arange(64, dtype=jnp.int32)
    row_rank = (pair_index - 8).astype(jnp.float32)
    col_rank = (pair_index - 36).astype(jnp.float32)
    log_base = math.log(10000.0)
    row_freq = jnp.where(
        (pair_index >= 8) & (pair_index < 36), jnp.exp(-2.0 * row_rank / 56.0 * log_base), 0.0
    )
    col_freq = jnp.where(pair_index >= 36, jnp.exp(-2.0 * col_rank / 56.0 * log_base), 0.0)
    angles = row_ids[..., None] * row_freq + col_ids[..., None] * col_freq
    angles = jnp.repeat(angles, 2, axis=-1)
    sign_table = jnp.where(jnp.arange(128, dtype=jnp.int32) % 2 == 0, -1.0, 1.0).astype(jnp.float32)
    return (jnp.cos(angles), jnp.sin(angles) * sign_table)


def rotate(values, cos_table, sin_table):
    paired = values.reshape(values.shape[:-1] + (values.shape[-1] // 2, 2))
    swapped = jnp.flip(paired, -1).reshape(values.shape)
    return values * cos_table + swapped * sin_table


def head_norm(projected, head_gain):
    squares = jnp.mean(projected * projected, -1, keepdims=True)
    return projected * lax.rsqrt(squares + norm_eps) * head_gain


def sigma_of(step_float):
    level = 1.0 - step_float / NSTEPS
    return time_shift * level / (1.0 + (time_shift - 1.0) * level)


def key_usable(text_len, key_count, text_tile, block_len):
    key_pos = jnp.arange(key_count, dtype=jnp.int32)
    owner_tile = key_pos // block_len
    offset = key_pos % block_len
    text_pos = owner_tile * text_tile + offset
    return jnp.logical_or(offset[None, :] >= text_tile, text_pos[None, :] < text_len[:, None])


def per_device(
    image_hidden,
    text_hidden,
    latents,
    step_index,
    anchor,
    text_len,
    mod_image,
    mod_text,
    mod_mlp,
    mod_final,
    qkv_image,
    qkv_text,
    proj_image,
    proj_text,
    qk_gain,
    mlp_expand,
    mlp_reduce,
    final_weight,
):
    requests, tile_rows, tile_cols, model_width = image_hidden.shape
    local_cols = qkv_image.shape[2]
    local_heads = local_cols // HEAD_DIM
    local_units = mlp_expand.shape[1]
    image_all, text_all = (
        lax.all_gather(image_hidden, "tensor", axis=2, tiled=True),
        lax.all_gather(text_hidden, "tensor", axis=1, tiled=True),
    )
    image_mod = modulate(image_all, mod_image[:, 0, None, None, :], mod_image[:, 1, None, None, :])
    text_mod = modulate(text_all, mod_text[:, 0, None, :], mod_text[:, 1, None, :])
    text_tile = text_mod.shape[1]
    image_count = tile_rows * GRID
    block_len = text_tile + image_count
    tile_index = lax.axis_index("tile")
    token_index = jnp.arange(image_count, dtype=jnp.int32)
    row_ids = (anchor[:, 0:1] + tile_index * tile_rows + token_index[None, :] // GRID).astype(
        jnp.float32
    )
    col_ids = (anchor[:, 1:2] + token_index[None, :] % GRID).astype(jnp.float32)
    cos_table, sin_table = rope_tables(row_ids, col_ids)
    cos_table = cos_table[:, :, None, :]
    sin_table = sin_table[:, :, None, :]
    image_qkv = jnp.dot(
        image_mod.reshape(requests * image_count, model_width),
        qkv_image.reshape(model_width, 3 * local_cols),
        preferred_element_type=jnp.float32,
    ).reshape(requests, image_count, 3, local_heads, HEAD_DIM)
    text_qkv = jnp.dot(
        text_mod.reshape(requests * text_tile, model_width),
        qkv_text.reshape(model_width, 3 * local_cols),
        preferred_element_type=jnp.float32,
    ).reshape(requests, text_tile, 3, local_heads, HEAD_DIM)
    query = jnp.concatenate(
        [
            head_norm(text_qkv[:, :, 0], qk_gain[1, 0]).astype(jnp.bfloat16),
            rotate(head_norm(image_qkv[:, :, 0], qk_gain[0, 0]), cos_table, sin_table).astype(
                jnp.bfloat16
            ),
        ],
        1,
    )
    keys = jnp.concatenate(
        [
            head_norm(text_qkv[:, :, 1], qk_gain[1, 1]).astype(jnp.bfloat16),
            rotate(head_norm(image_qkv[:, :, 1], qk_gain[0, 1]), cos_table, sin_table).astype(
                jnp.bfloat16
            ),
        ],
        1,
    )
    values = jnp.concatenate([text_qkv[:, :, 2], image_qkv[:, :, 2]], 1).astype(jnp.bfloat16)
    score_scale = 1.0 / math.sqrt(HEAD_DIM)
    keys_all, values_all = (
        lax.all_gather(keys, "tile", axis=1, tiled=True),
        lax.all_gather(values, "tile", axis=1, tiled=True),
    )
    usable = key_usable(text_len, keys_all.shape[1], text_tile, block_len)[:, None, None, :]
    scores = (
        jnp.einsum("rqhd,rkhd->rhqk", query, keys_all, preferred_element_type=jnp.float32)
        * score_scale
    )
    row_top = jnp.max(jnp.where(usable, scores, -jnp.inf), -1, keepdims=True)
    weights_raw = jnp.where(usable, jnp.exp(scores - row_top), 0.0)
    weight_sum = jnp.sum(weights_raw, -1, keepdims=True)
    accum = jnp.einsum(
        "rhqk,rkhd->rhqd",
        weights_raw.astype(jnp.bfloat16),
        values_all,
        preferred_element_type=jnp.float32,
    )
    attended = (accum / weight_sum).transpose(0, 2, 1, 3).astype(jnp.bfloat16)
    text_term = jnp.dot(
        attended[:, :text_tile].reshape(requests * text_tile, local_cols),
        proj_text,
        preferred_element_type=jnp.float32,
    ).reshape(requests, text_tile, model_width)
    image_term = jnp.dot(
        attended[:, text_tile:].reshape(requests * image_count, local_cols),
        proj_image,
        preferred_element_type=jnp.float32,
    ).reshape(requests, tile_rows, GRID, model_width)
    image_gate = mod_image[:, 2, None, None, :]
    image_sum, text_sum = (
        lax.psum_scatter(image_term, "tensor", scatter_dimension=2, tiled=True),
        lax.psum_scatter(text_term, "tensor", scatter_dimension=1, tiled=True),
    )
    image_mid = (image_hidden.astype(jnp.float32) + image_gate * image_sum).astype(jnp.bfloat16)
    mlp_mod = modulate(image_mid, mod_mlp[:, 0, None, None, :], mod_mlp[:, 1, None, None, :])
    piece = lax.all_gather(mlp_mod, "tensor", axis=2, tiled=True)
    grown = jnp.dot(piece.reshape(-1, model_width), mlp_expand, preferred_element_type=jnp.float32)
    activated = (
        jax.nn.gelu(grown, approximate=True)
        .astype(jnp.bfloat16)
        .reshape(piece.shape[:-1] + (local_units,))
    )
    text_out = (text_hidden.astype(jnp.float32) + mod_text[:, 2, None, :] * text_sum).astype(
        jnp.bfloat16
    )
    mlp_term = jnp.dot(
        activated.reshape(requests * image_count, local_units),
        mlp_reduce,
        preferred_element_type=jnp.float32,
    ).reshape(requests, tile_rows, GRID, model_width)
    mlp_sum = lax.psum_scatter(mlp_term, "tensor", scatter_dimension=2, tiled=True)
    image_out = (image_mid.astype(jnp.float32) + mod_mlp[:, 2, None, None, :] * mlp_sum).astype(
        jnp.bfloat16
    )
    final_in = modulate(image_out, mod_final[:, 0, None, None, :], mod_final[:, 1, None, None, :])
    velocity = jnp.dot(
        final_in.reshape(requests * tile_rows * tile_cols, model_width),
        final_weight,
        preferred_element_type=jnp.float32,
    ).reshape(requests, tile_rows, tile_cols * final_weight.shape[1])
    step_float = step_index.astype(jnp.float32)
    time_delta = sigma_of(step_float + 1.0) - sigma_of(step_float)
    latents_next = latents + time_delta[:, None, None] * velocity
    latents_ext = padded(latents_next, (("tile", 1),), 1)
    return (image_out, text_out, latents_ext)


def solution(mesh):
    return jax.shard_map(
        per_device,
        mesh=mesh,
        in_specs=(
            P(None, "tile", "tensor", None),
            P(None, ("tile", "tensor"), None),
            P(None, "tile", "tensor"),
            P(),
            P(),
            P(),
            P(),
            P(),
            P(),
            P(),
            P(None, None, "tensor"),
            P(None, None, "tensor"),
            P("tensor", None),
            P("tensor", None),
            P(),
            P(None, "tensor"),
            P("tensor", None),
            P(),
        ),
        out_specs=(
            P(None, "tile", "tensor", None),
            P(None, ("tile", "tensor"), None),
            P(None, "tile", "tensor"),
        ),
        check_vma=False,
    )
```

profile of v0, /device:TPU:32, one launch (start us, length us, event | category | flops | bytes accessed | tf_op | source)
XLA Modules:
  0.0 585.7 jit_solution(4433946694455913558)
XLA Ops:
  10.8 4.3 copy.66
  18.5 4.3 copy.63
  25.6 36.5 %all-gather.6.cloned.1.call-done = bf16[8,32,3072]{2,0,1:T(8,128)(2,1)} async-done(((bf16[8,2,3072]{2,0,1:T(8,128)(2,1)}), bf16[8,32,3072]{2,0,1:T(8,128)(2,1)}) %all-gather.6.cloned.1.call-update) | async-done | bytes 1572880 | tf_op jit(solution)/shard_map/all_gather | solution.py:104
  62.1 1.8 convert_reduce_fusion.1
  63.9 2.0 fusion.13
  65.9 2.8 fusion.38
  70.8 46.7 %all-gather.8.cloned.1.call-done = bf16[8,2,32,3072]{3,0,1,2:T(8,128)(2,1)} async-done(((bf16[8,2,2,3072]{3,0,1,2:T(8,128)(2,1)}), bf16[8,2,32,3072]{3,0,1,2:T(8,128)(2,1)}) %all-gather.8.cloned.1.call-update) | async-done | bytes 3145744 | tf_op jit(solution)/shard_map/all_gather | solution.py:103
  117.5 5.4 convert_reduce_fusion
  122.9 3.2 fusion.3
  126.1 7.0 %fusion.6 = bf16[8,2,32,3072]{3,2,1,0:T(8,128)(2,1)S(1)} fusion(f32[8,3072]{1,0:T(8,128)S(1)} %get-tuple-element.32, f32[8,2,32]{2,1,0:T(2,128)S(1)} %add_rsqrt_fusion.3, f32[8,2,32]{2,1,0:T(2,128)S(1)} %broadcast_multiply_fusion.1, f32[8,3072]{1,0:T(8,128)S(1)} %get-tuple-element.33, bf16[8,2,32,3072]{3,0,1,2:T(8,128)(2,1)S(1)} %copy-done.1), kind=kLoop, calls=%fused_computation.8 | loop fusion | flops 9437184 | bytes 6492160 | tf_op jit(solution)/shard_map/convert_element_type | solution.py:36
  135.9 2.0 copy.74
  137.9 2.0 multiply_multiply_fusion.1
  139.9 1.9 rev.8
  141.8 1.9 copy.75
  144.7 2.0 multiply_multiply_fusion.2
  146.7 1.9 rev.7
  156.1 36.4 %all-gather.10.cloned.1.call-done = bf16[8,1536,1,128]{3,1,0,2:T(8,128)(2,1)} async-done(((bf16[8,96,1,128]{3,1,0,2:T(8,128)(2,1)}), bf16[8,1536,1,128]{3,1,0,2:T(8,128)(2,1)}) %all-gather.10.cloned.1.call-update) | async-done | bytes 3145744 | tf_op jit(solution)/shard_map/all_gather | solution.py:151
  192.5 3.0 fusion.19
  195.6 3.0 fusion.132
  198.5 36.0 %all-gather.12.cloned.1.call-done = bf16[8,1536,1,128]{3,1,0,2:T(8,128)(2,1)} async-done(((bf16[8,96,1,128]{3,1,0,2:T(8,128)(2,1)}), bf16[8,1536,1,128]{3,1,0,2:T(8,128)(2,1)}) %all-gather.12.cloned.1.call-update) | async-done | bytes 3145744 | tf_op jit(solution)/shard_map/all_gather | solution.py:152
  234.5 3.5 fusion.53
  238.7 3.6 fusion.68
  243.3 84.6 %reduce-scatter.4.cloned.1.call-done = f32[8,2,2,3072]{3,0,1,2:T(8,128)} async-done(((f32[8,2,32,3072]{3,0,1,2:T(8,128)}), f32[8,2,2,3072]{3,0,1,2:T(8,128)}) %reduce-scatter.4.cloned.1.call-update) | async-done | bytes 393232 | tf_op jit(solution)/shard_map/reduce_scatter | solution.py:181
  330.5 52.7 %all-gather.14.cloned.1.call-done = bf16[8,2,32,3072]{3,0,1,2:T(8,128)(2,1)} async-done(((bf16[8,2,2,3072]{3,0,1,2:T(8,128)(2,1)}), bf16[8,2,32,3072]{3,0,1,2:T(8,128)(2,1)}) %all-gather.14.cloned.1.call-update) | async-done | bytes 3145744 | tf_op jit(solution)/shard_map/all_gather | solution.py:186
  383.2 5.3 copy.79
  388.4 8.8 %fusion.83 = f32[512,3072]{1,0:T(8,128)} fusion(bf16[384,3072]{1,0:T(8,128)(2,1)S(1)} %copy-done, bf16[512,3072]{1,0:T(8,128)(2,1)} %bitcast.160, bf16[3072,384]{1,0:T(8,128)(2,1)} %param.33), kind=kOutput, calls=%fused_computation.76 | convolution fusion | flops 2417688576 | bytes 14155776 | tf_op jit(solution)/shard_map/dot_general | solution.py:196
  397.2 9.1 %copy.80 = f32[8,2,32,3072]{3,0,1,2:T(8,128)} copy(f32[8,2,32,3072]{3,2,1,0:T(8,128)} %bitcast.158) | data formatting | bytes 12582912 | tf_op jit(solution)/shard_map/reshape | solution.py:200
  407.5 2.3 fusion.66
  410.9 80.8 %reduce-scatter.6.cloned.1.call-done = f32[8,2,2,3072]{3,0,1,2:T(8,128)} async-done(((f32[8,2,32,3072]{3,0,1,2:T(8,128)}), f32[8,2,2,3072]{3,0,1,2:T(8,128)}) %reduce-scatter.6.cloned.1.call-update) | async-done | bytes 393232 | tf_op jit(solution)/shard_map/reduce_scatter | solution.py:201
  494.0 1.9 collective-permute-start
  495.9 3.6 collective-permute-start.1
  499.5 76.0 %reduce-scatter.8.cloned.1.call-done = f32[8,2,3072]{2,0,1:T(8,128)} async-done(((f32[8,32,3072]{2,0,1:T(8,128)}), f32[8,2,3072]{2,0,1:T(8,128)}) %reduce-scatter.8.cloned.1.call-update) | async-done | bytes 196624 | tf_op jit(solution)/shard_map/reduce_scatter | solution.py:182
  (124 shorter events, 34.9 us)
Async XLA Ops:
  7.2 381.3 %copy-start = (bf16[384,3072]{1,0:T(8,128)(2,1)S(1)}, bf16[384,3072]{1,0:T(8,128)(2,1)}, u32[]{:S(2)}) copy-start(bf16[384,3072]{1,0:T(8,128)(2,1)} %param.34) | copy-start | bytes 7077892
  7.2 7.9 %copy-start.16 = (f32[2,2,128]{2,1,0:T(2,128)S(1)}, f32[2,2,128]{2,1,0:T(2,128)}, u32[]{:S(2)}) copy-start(f32[2,2,128]{2,1,0:T(2,128)} %param.32) | copy-start | bytes 6148
  7.2 8.2 %copy-start.17 = (s32[8,2]{0,1:T(2,128)S(1)}, s32[8,2]{0,1:T(2,128)}, u32[]{:S(2)}) copy-start(s32[8,2]{0,1:T(2,128)} %param.22) | copy-start | bytes 196
  7.2 54.9 %all-gather.6.cloned.1.call-start = ((), (), s32[]{:S(2)}) async-start(), calls=%async_computation.3 | async-start | bytes 1671168 | tf_op jit(solution)/shard_map/all_gather | solution.py:104
  9.0 108.5 %all-gather.8.cloned.1.call-start = ((), (), s32[]{:S(2)}) async-start(), calls=%async_computation.4 | async-start | bytes 3342336 | tf_op jit(solution)/shard_map/all_gather | solution.py:103
  10.7 181.8 %all-gather.10.cloned.1.call-start = ((), (), s32[]{:S(2)}) async-start(), calls=%async_computation.5 | async-start | bytes 3342336 | tf_op jit(solution)/shard_map/all_gather | solution.py:151
  17.5 5.7 copy-start.11
  62.1 3.8 copy-start.2
  68.7 0.8 copy-start.4
  117.5 5.4 copy-start.1
  126.0 7.1 %copy-start.3 = (bf16[3072,3,128]{0,2,1:T(8,128)(2,1)S(1)}, bf16[3072,3,128]{0,2,1:T(8,128)(2,1)}, u32[]{:S(2)}) copy-start(bf16[3072,3,128]{0,2,1:T(8,128)(2,1)} %copy.66) | copy-start | bytes 7077892
  152.7 81.8 %all-gather.12.cloned.1.call-start = ((), (), s32[]{:S(2)}) async-start(), calls=%async_computation.6 | async-start | bytes 3342336 | tf_op jit(solution)/shard_map/all_gather | solution.py:152
  154.4 173.5 %reduce-scatter.4.cloned.1.call-start = ((), (), s32[]{:S(2)}) async-start(), calls=%async_computation.7 | async-start | bytes 6684672 | tf_op jit(solution)/shard_map/reduce_scatter | solution.py:181
  234.5 4.2 copy-start.5
  238.0 0.7 copy-start.14
  242.3 1.0 copy-start.12
  242.3 85.6 %copy-start.6 = (bf16[8,2,2,3072]{3,2,1,0:T(2,128)(2,1)S(1)}, bf16[8,2,2,3072]{3,2,1,0:T(2,128)(2,1)}, u32[]{:S(2)}) copy-start(bf16[8,2,2,3072]{3,2,1,0:T(2,128)(2,1)} %param.18) | copy-start | bytes 589828
  242.3 85.6 %copy-start.8 = (f32[8,3072]{1,0:T(8,128)S(1)}, f32[8,3072]{1,0:T(8,128)}, u32[]{:S(2)}) copy-start(f32[8,3072]{1,0:T(8,128)} %get-tuple-element.31) | copy-start | bytes 294916
  242.4 140.8 %all-gather.14.cloned.1.call-start = ((), (), s32[]{:S(2)}) async-start(), calls=%async_computation.8 | async-start | bytes 3342336 | tf_op jit(solution)/shard_map/all_gather | solution.py:186
  330.2 161.5 %reduce-scatter.6.cloned.1.call-start = ((), (), s32[]{:S(2)}) async-start(), calls=%async_computation.9 | async-start | bytes 6684672 | tf_op jit(solution)/shard_map/reduce_scatter | solution.py:201
  406.3 1.2 copy-start.7
  406.3 169.2 %reduce-scatter.8.cloned.1.call-start = ((), (), s32[]{:S(2)}) async-start(), calls=%async_computation.10 | async-start | bytes 3342336 | tf_op jit(solution)/shard_map/reduce_scatter | solution.py:182
  407.5 2.3 copy-start.18
  409.7 0.9 copy-start.13
  409.7 83.8 %copy-start.9 = (bf16[3072,64]{0,1:T(8,128)(2,1)S(1)}, bf16[3072,64]{0,1:T(8,128)(2,1)}, u32[]{:S(2)}) copy-start(bf16[3072,64]{0,1:T(8,128)(2,1)} %param.35) | copy-start | bytes 1179652
  409.8 84.1 %copy-start.15 = (f32[8,2,128]{2,1,0:T(2,128)S(1)}, f32[8,2,128]{2,1,0:T(2,128)}, u32[]{:S(2)}) copy-start(f32[8,2,128]{2,1,0:T(2,128)} %param.20) | copy-start | bytes 24580
  409.8 165.8 %copy-start.10 = (f32[8,3072]{1,0:T(8,128)S(1)}, f32[8,3072]{1,0:T(8,128)}, u32[]{:S(2)}) copy-start(f32[8,3072]{1,0:T(8,128)} %get-tuple-element.25) | copy-start | bytes 294916
  494.0 84.2 %collective-permute-start = (f32[8,1,128]{2,1,0:T(1,128)S(1)}, f32[8,1,128]{2,1,0:T(1,128)S(1)}, u32[]{:S(2)}, u32[]{:S(2)}) collective-permute-start(f32[8,1,128]{2,1,0:T(1,128)S(1)} %get-tuple-element.38), channel_id=1, source_target_pairs={{0,16},{16,32},{32,48},{48,64},{64,80},{80,96},{96,112},{112,128},... | collective-permute-start | bytes 12296 | tf_op jit(solution)/shard_map/ppermute | solution.py:21
  495.9 82.3 %collective-permute-start.1 = (f32[8,1,128]{2,1,0:T(1,128)S(1)}, f32[8,1,128]{2,1,0:T(1,128)S(1)}, u32[]{:S(2)}, u32[]{:S(2)}) collective-permute-start(f32[8,1,128]{2,1,0:T(1,128)S(1)} %get-tuple-element.39), channel_id=1, source_target_pairs={{16,0},{32,16},{48,32},{64,48},{80,64},{96,80},{112,96},{128,112},... | collective-permute-start | bytes 12296 | tf_op jit(solution)/shard_map/ppermute | solution.py:22
Sparse Core Ops, SparseCore 0:
  10.5 51.5 all-gather.5
  65.1 52.3 all-gather.7
  152.8 39.6 all-gather.9
  194.8 39.6 all-gather.11
  242.5 85.3 reduce-scatter.3
  330.8 52.3 all-gather.13
  406.5 85.2 reduce-scatter.5
  495.3 80.1 reduce-scatter.7
where the time goes:
time: 587 us; the launch traced here: 586 us
  waiting for transfers between devices  450 us (77%)
  local copies, waits for them, and re-layouts  47.8 us (8%)
  other arithmetic  41.3 us (7%)
  matrix products  26 us (4%)
  between operations  14.5 us (2%)
  starting transfers between devices  6.11 us (1%)
    reduce_scatter x1, waiting for transfers between devices, per_device(): lax.psum_scatter(image_term, 'tensor', scatter_dimension=2, tiled=True)  84.6 us
    reduce_scatter x1, waiting for transfers between devices, per_device(): lax.psum_scatter(mlp_term, 'tensor', scatter_dimension=2, tiled=True)  80.8 us
    reduce_scatter x1, waiting for transfers between devices, per_device(): lax.psum_scatter(text_term, 'tensor', scatter_dimension=1, tiled=True)  76 us
    all_gather x1, waiting for transfers between devices, per_device(): piece = lax.all_gather(mlp_mod, 'tensor', axis=2, tiled=True)  52.7 us
    all_gather x1, waiting for transfers between devices, per_device(): lax.all_gather(image_hidden, 'tensor', axis=2, tiled=True)  46.7 us
    all_gather x1, waiting for transfers between devices, per_device(): lax.all_gather(text_hidden, 'tensor', axis=1, tiled=True)  36.5 us
    all_gather x1, waiting for transfers between devices, per_device(): lax.all_gather(keys, 'tile', axis=1, tiled=True)  36.4 us
    all_gather x1, waiting for transfers between devices, per_device(): lax.all_gather(values, 'tile', axis=1, tiled=True)  36 us
  transfers between devices with their start and end apart: 10, of which 8 were waited for; matrix products, arithmetic and copies ran while one was open for 7% of the time, Pallas kernels for 0%

commit v1 on v0

--- a/solution.py
+++ b/solution.py
@@ -99,9 +99,30 @@
     local_cols = qkv_image.shape[2]
     local_heads = local_cols // HEAD_DIM
     local_units = mlp_expand.shape[1]
+
+    def attach_the_sheet(axis_k, panel, comm_axis):
+        full_n = lax.axis_size(comm_axis)
+        vals = []
+        for j0 in [*range(full_n)]:
+            vals.append((j0, (j0 + 1) % full_n))
+        leaves = []
+        for j0 in tuple(range(full_n)):
+            leaves.append((j0, (j0 - 1) % full_n))
+        field_out, right_arr = ([panel], [panel])
+        for _ in range(full_n // 2):
+            field_out.append(lax.ppermute(field_out[-1], axis_name=comm_axis, perm=vals))
+        for _ in [*range((full_n - 1) // 2)]:
+            outer = lax.ppermute(right_arr[-1], perm=leaves, axis_name=comm_axis)
+            right_arr.append(outer)
+        all_rows = jnp.concatenate([*field_out[::-1], *right_arr[1:]], axis_k)
+        formed = jnp.roll(
+            all_rows, (lax.axis_index(comm_axis) - full_n // 2) * panel.shape[axis_k], axis_k
+        )
+        return formed
+
     image_all, text_all = (
         lax.all_gather(image_hidden, "tensor", axis=2, tiled=True),
-        lax.all_gather(text_hidden, "tensor", axis=1, tiled=True),
+        attach_the_sheet(1, text_hidden, "tensor"),
     )
     image_mod = modulate(image_all, mod_image[:, 0, None, None, :], mod_image[:, 1, None, None, :])
     text_mod = modulate(text_all, mod_text[:, 0, None, :], mod_text[:, 1, None, :])

time: 587 us -> 594 us (1.012); the launches traced: 586 us -> 583 us
  waiting for transfers between devices: 450 us -> 383 us
  starting transfers between devices: 6.11 us -> 44.1 us
  local copies, waits for them, and re-layouts: 47.8 us -> 67.8 us
    all_gather x1, waiting for transfers between devices: 46.7 us -> 0.01 us  [per_device(): lax.all_gather(image_hidden, 'tensor', axis=2, tiled=True)]
    ppermute x0 -> x15, starting transfers between devices: none -> 38 us  [the longest x7 36.2 us: attach_the_sheet(): outer = lax.ppermute(right_arr[-1], perm=leaves, axis_name=comm_axis)]
    all_gather x1 -> x0, waiting for transfers between devices: 36.5 us -> none  [per_device(): lax.all_gather(text_hidden, 'tensor', axis=1, tiled=True)]
    concatenate x0 -> x1, local copies, waits for them, and re-layouts: none -> 21.5 us  [attach_the_sheet(): jnp.roll(all_rows, (lax.axis_index(comm_axis) - full_n // 2) * panel.shap...]
    ppermute x0 -> x15, waiting for transfers between devices: none -> 17.8 us  [the longest x8 15.8 us: attach_the_sheet(): lax.ppermute(field_out[-1], axis_name=comm_axis, perm=vals)]
    unnamed x45 -> x72, local copies, waits for them, and re-layouts: 17.6 us -> 15.3 us
  transfers between devices with their start and end apart: 10 -> 24, of which waited for: 8 -> 12; matrix products, arithmetic and copies ran while one was open for 7% -> 12% of each run, Pallas kernels for 0% -> 0%
where the time goes in v1:
time: 594 us; the launch traced here: 583 us
  waiting for transfers between devices  383 us (64%)
  local copies, waits for them, and re-layouts  67.8 us (11%)
  other arithmetic  46.6 us (8%)
  starting transfers between devices  44.1 us (7%)
  matrix products  26.2 us (4%)
  between operations  15.1 us (3%)
    reduce_scatter x1, waiting for transfers between devices, per_device(): lax.psum_scatter(image_term, 'tensor', scatter_dimension=2, tiled=True)  84 us
    reduce_scatter x1, waiting for transfers between devices, per_device(): lax.psum_scatter(mlp_term, 'tensor', scatter_dimension=2, tiled=True)  80.2 us
    reduce_scatter x1, waiting for transfers between devices, per_device(): lax.psum_scatter(text_term, 'tensor', scatter_dimension=1, tiled=True)  75.1 us
    all_gather x1, waiting for transfers between devices, per_device(): piece = lax.all_gather(mlp_mod, 'tensor', axis=2, tiled=True)  52.7 us
    all_gather x1, waiting for transfers between devices, per_device(): lax.all_gather(keys, 'tile', axis=1, tiled=True)  37.2 us
    ppermute x7, starting transfers between devices, attach_the_sheet(): outer = lax.ppermute(right_arr[-1], perm=leaves, axis_name=comm_axis)  36.2 us
    all_gather x1, waiting for transfers between devices, per_device(): lax.all_gather(values, 'tile', axis=1, tiled=True)  36 us
    concatenate x1, local copies, waits for them, and re-layouts, attach_the_sheet(): jnp.roll(all_rows, (lax.axis_index(comm_axis) - full_n // 2) * panel.shap...  21.5 us
  transfers between devices with their start and end apart: 24, of which 12 were waited for; matrix products, arithmetic and copies ran while one was open for 12% of the time, Pallas kernels for 0%

profile of v1, /device:TPU:32, one launch (start us, length us, event | category | flops | bytes accessed | tf_op | source)
XLA Modules:
  0.0 583.1 jit_solution(13688114268853289919)
XLA Ops:
  10.7 3.9 collective-permute-start.8
  18.8 5.4 collective-permute-start.9
  24.2 2.5 collective-permute-done.1
  26.8 5.4 collective-permute-start.10
  32.2 2.8 collective-permute-done.2
  35.0 5.4 collective-permute-start.11
  42.9 5.4 collective-permute-start.12
  51.9 4.3 copy.58
  56.2 4.4 copy.61
  60.6 5.4 collective-permute-start.13
  69.6 5.3 collective-permute-start.14
  77.5 5.6 collective-permute-done.7
  83.1 21.5 %concatenate.31 = bf16[8,64,3072]{2,1,0:T(8,128)(2,1)} concatenate(bf16[8,2,3072]{2,1,0:T(2,128)(2,1)S(1)} %collective-permute-done.7, bf16[8,2,3072]{2,1,0:T(2,128)(2,1)} %collective-permute-done.6, bf16[8,2,3072]{2,1,0:T(2,128)(2,1)} %collective-permute-done.5, bf16[8,2,3072]{2,1,0:T(2,128)(2,1)} %copy-done.22, bf16[8,2,3072]{2,1,0:T(2,128)(2,1)} %copy-done.20, ...), dimensions={1} | concatenate | bytes 6291456 | tf_op jit(solution)/shard_map/jit(_roll_dynamic)/concatenate | solution.py:118
  106.9 2.5 fusion.13
  109.4 2.9 fusion.38
  113.9 5.4 convert_reduce_fusion
  119.3 3.2 fusion.3
  122.5 7.1 %fusion.6 = bf16[8,2,32,3072]{3,2,1,0:T(8,128)(2,1)S(1)} fusion(f32[8,3072]{1,0:T(8,128)S(1)} %copy-done.12, f32[8,2,32]{2,1,0:T(2,128)S(1)} %add_rsqrt_fusion, f32[8,2,32]{2,1,0:T(2,128)S(1)} %broadcast_multiply_fusion, f32[8,3072]{1,0:T(8,128)S(1)} %copy-done.13, bf16[8,2,32,3072]{3,0,1,2:T(8,128)(2,1)S(1)} %copy-done.1), kind=kLoop, calls=%fused_computation.8 | loop fusion | flops 9437184 | bytes 6492160 | tf_op jit(solution)/shard_map/convert_element_type | solution.py:36
  151.8 37.2 %all-gather.7.cloned.1.call-done = bf16[8,1536,1,128]{3,1,0,2:T(8,128)(2,1)} async-done(((bf16[8,96,1,128]{3,1,0,2:T(8,128)(2,1)}), bf16[8,1536,1,128]{3,1,0,2:T(8,128)(2,1)}) %all-gather.7.cloned.1.call-update) | async-done | bytes 3145744 | tf_op jit(solution)/shard_map/all_gather | solution.py:172
  189.0 3.1 fusion.19
  192.2 3.0 fusion.134
  195.1 36.0 %all-gather.9.cloned.1.call-done = bf16[8,1536,1,128]{3,1,0,2:T(8,128)(2,1)} async-done(((bf16[8,96,1,128]{3,1,0,2:T(8,128)(2,1)}), bf16[8,1536,1,128]{3,1,0,2:T(8,128)(2,1)}) %all-gather.9.cloned.1.call-update) | async-done | bytes 3145744 | tf_op jit(solution)/shard_map/all_gather | solution.py:173
  231.1 3.5 fusion.54
  235.3 3.6 fusion.69
  240.5 84.0 %reduce-scatter.4.cloned.1.call-done = f32[8,2,2,3072]{3,0,1,2:T(8,128)} async-done(((f32[8,2,32,3072]{3,0,1,2:T(8,128)}), f32[8,2,2,3072]{3,0,1,2:T(8,128)}) %reduce-scatter.4.cloned.1.call-update) | async-done | bytes 393232 | tf_op jit(solution)/shard_map/reduce_scatter | solution.py:202
  327.1 52.7 %all-gather.11.cloned.1.call-done = bf16[8,2,32,3072]{3,0,1,2:T(8,128)(2,1)} async-done(((bf16[8,2,2,3072]{3,0,1,2:T(8,128)(2,1)}), bf16[8,2,32,3072]{3,0,1,2:T(8,128)(2,1)}) %all-gather.11.cloned.1.call-update) | async-done | bytes 3145744 | tf_op jit(solution)/shard_map/all_gather | solution.py:207
  379.8 5.2 copy.71
  385.1 8.8 %fusion.84 = f32[512,3072]{1,0:T(8,128)} fusion(bf16[384,3072]{1,0:T(8,128)(2,1)S(1)} %copy-done, bf16[512,3072]{1,0:T(8,128)(2,1)} %bitcast.160, bf16[3072,384]{1,0:T(8,128)(2,1)} %param.33), kind=kOutput, calls=%fused_computation.77 | convolution fusion | flops 2417688576 | bytes 14155776 | tf_op jit(solution)/shard_map/dot_general | solution.py:217
  393.8 9.1 %copy.72 = f32[8,2,32,3072]{3,0,1,2:T(8,128)} copy(f32[8,2,32,3072]{3,2,1,0:T(8,128)} %bitcast.158) | data formatting | bytes 12582912 | tf_op jit(solution)/shard_map/reshape | solution.py:221
  408.4 80.2 %reduce-scatter.6.cloned.1.call-done = f32[8,2,2,3072]{3,0,1,2:T(8,128)} async-done(((f32[8,2,32,3072]{3,0,1,2:T(8,128)}), f32[8,2,2,3072]{3,0,1,2:T(8,128)}) %reduce-scatter.6.cloned.1.call-update) | async-done | bytes 393232 | tf_op jit(solution)/shard_map/reduce_scatter | solution.py:222
  493.7 3.6 collective-permute-start.16
  497.4 75.1 %reduce-scatter.8.cloned.1.call-done = f32[8,2,3072]{2,0,1:T(8,128)} async-done(((f32[8,32,3072]{2,0,1:T(8,128)}), f32[8,2,3072]{2,0,1:T(8,128)}) %reduce-scatter.8.cloned.1.call-update) | async-done | bytes 196624 | tf_op jit(solution)/shard_map/reduce_scatter | solution.py:203
  (176 shorter events, 64.4 us)
Async XLA Ops:
  7.2 377.9 %copy-start = (bf16[384,3072]{1,0:T(8,128)(2,1)S(1)}, bf16[384,3072]{1,0:T(8,128)(2,1)}, u32[]{:S(2)}) copy-start(bf16[384,3072]{1,0:T(8,128)(2,1)} %param.34) | copy-start | bytes 7077892
  7.2 106.7 %all-gather.5.cloned.1.call-start = ((), (), s32[]{:S(2)}) async-start(), calls=%async_computation.3 | async-start | bytes 3342336 | tf_op jit(solution)/shard_map/all_gather | solution.py:124
  9.1 180.0 %all-gather.7.cloned.1.call-start = ((), (), s32[]{:S(2)}) async-start(), calls=%async_computation.4 | async-start | bytes 3342336 | tf_op jit(solution)/shard_map/all_gather | solution.py:172
  9.1 9.6 %collective-permute-start = (bf16[8,2,3072]{2,1,0:T(2,128)(2,1)}, bf16[8,2,3072]{2,1,0:T(2,128)(2,1)S(1)}, u32[]{:S(2)}, u32[]{:S(2)}) collective-permute-start(bf16[8,2,3072]{2,1,0:T(2,128)(2,1)} %param.19), channel_id=1, source_target_pairs={{0,1},{1,2},{2,3},{3,4},{4,5},{5,6},{6,7},{7,8},{8,9},{9,10},{10,1... | collective-permute-start | bytes 294920 | tf_op jit(solution)/shard_map/ppermute | solution.py:113
  10.7 8.1 %collective-permute-start.8 = (bf16[8,2,3072]{2,1,0:T(2,128)(2,1)}, bf16[8,2,3072]{2,1,0:T(2,128)(2,1)S(1)}, u32[]{:S(2)}, u32[]{:S(2)}) collective-permute-start(bf16[8,2,3072]{2,1,0:T(2,128)(2,1)} %param.19), channel_id=1, source_target_pairs={{0,15},{1,0},{2,1},{3,2},{4,3},{5,4},{6,5},{7,6},{8,7},{9,8},{10,9... | collective-permute-start | bytes 294920 | tf_op jit(solution)/shard_map/ppermute | solution.py:115
  18.7 41.9 %copy-start.14 = (bf16[8,2,3072]{2,1,0:T(2,128)(2,1)}, bf16[8,2,3072]{2,1,0:T(2,128)(2,1)S(1)}, u32[]{:S(2)}) copy-start(bf16[8,2,3072]{2,1,0:T(2,128)(2,1)S(1)} %collective-permute-done) | copy-start | bytes 294916
  18.7 8.0 %collective-permute-start.1 = (bf16[8,2,3072]{2,1,0:T(2,128)(2,1)S(1)}, bf16[8,2,3072]{2,1,0:T(2,128)(2,1)S(1)}, u32[]{:S(2)}, u32[]{:S(2)}) collective-permute-start(bf16[8,2,3072]{2,1,0:T(2,128)(2,1)S(1)} %collective-permute-done), channel_id=1, source_target_pairs={{0,1},{1,2},{2,3},{3,4},{4,5},{5,6},{6,7},{7,8},{8,9},{9,10},{10,1... | collective-permute-start | bytes 294920 | tf_op jit(solution)/shard_map/ppermute | solution.py:113
  18.8 41.8 %copy-start.15 = (bf16[8,2,3072]{2,1,0:T(2,128)(2,1)}, bf16[8,2,3072]{2,1,0:T(2,128)(2,1)S(1)}, u32[]{:S(2)}) copy-start(bf16[8,2,3072]{2,1,0:T(2,128)(2,1)S(1)} %collective-permute-done.8) | copy-start | bytes 294916
  18.8 7.9 %collective-permute-start.9 = (bf16[8,2,3072]{2,1,0:T(2,128)(2,1)S(1)}, bf16[8,2,3072]{2,1,0:T(2,128)(2,1)S(1)}, u32[]{:S(2)}, u32[]{:S(2)}) collective-permute-start(bf16[8,2,3072]{2,1,0:T(2,128)(2,1)S(1)} %collective-permute-done.8), channel_id=1, source_target_pairs={{0,15},{1,0},{2,1},{3,2},{4,3},{5,4},{6,5},{7,6},{8,7},{9,8},{10,9... | collective-permute-start | bytes 294920 | tf_op jit(solution)/shard_map/ppermute | solution.py:115
  26.7 8.2 %collective-permute-start.2 = (bf16[8,2,3072]{2,1,0:T(2,128)(2,1)S(1)}, bf16[8,2,3072]{2,1,0:T(2,128)(2,1)S(1)}, u32[]{:S(2)}, u32[]{:S(2)}) collective-permute-start(bf16[8,2,3072]{2,1,0:T(2,128)(2,1)S(1)} %collective-permute-done.1), channel_id=1, source_target_pairs={{0,1},{1,2},{2,3},{3,4},{4,5},{5,6},{6,7},{7,8},{8,9},{9,10},{10,1... | collective-permute-start | bytes 294920 | tf_op jit(solution)/shard_map/ppermute | solution.py:113
  26.8 8.3 %collective-permute-start.10 = (bf16[8,2,3072]{2,1,0:T(2,128)(2,1)S(1)}, bf16[8,2,3072]{2,1,0:T(2,128)(2,1)S(1)}, u32[]{:S(2)}, u32[]{:S(2)}) collective-permute-start(bf16[8,2,3072]{2,1,0:T(2,128)(2,1)S(1)} %collective-permute-done.9), channel_id=1, source_target_pairs={{0,15},{1,0},{2,1},{3,2},{4,3},{5,4},{6,5},{7,6},{8,7},{9,8},{10,9... | collective-permute-start | bytes 294920 | tf_op jit(solution)/shard_map/ppermute | solution.py:115
  34.9 7.9 %collective-permute-start.3 = (bf16[8,2,3072]{2,1,0:T(2,128)(2,1)S(1)}, bf16[8,2,3072]{2,1,0:T(2,128)(2,1)S(1)}, u32[]{:S(2)}, u32[]{:S(2)}) collective-permute-start(bf16[8,2,3072]{2,1,0:T(2,128)(2,1)S(1)} %collective-permute-done.2), channel_id=1, source_target_pairs={{0,1},{1,2},{2,3},{3,4},{4,5},{5,6},{6,7},{7,8},{8,9},{9,10},{10,1... | collective-permute-start | bytes 294920 | tf_op jit(solution)/shard_map/ppermute | solution.py:113
  35.0 7.9 %collective-permute-start.11 = (bf16[8,2,3072]{2,1,0:T(2,128)(2,1)S(1)}, bf16[8,2,3072]{2,1,0:T(2,128)(2,1)S(1)}, u32[]{:S(2)}, u32[]{:S(2)}) collective-permute-start(bf16[8,2,3072]{2,1,0:T(2,128)(2,1)S(1)} %collective-permute-done.10), channel_id=1, source_target_pairs={{0,15},{1,0},{2,1},{3,2},{4,3},{5,4},{6,5},{7,6},{8,7},{9,8},{10,9... | collective-permute-start | bytes 294920 | tf_op jit(solution)/shard_map/ppermute | solution.py:115
  42.9 7.9 %collective-permute-start.4 = (bf16[8,2,3072]{2,1,0:T(2,128)(2,1)S(1)}, bf16[8,2,3072]{2,1,0:T(2,128)(2,1)S(1)}, u32[]{:S(2)}, u32[]{:S(2)}) collective-permute-start(bf16[8,2,3072]{2,1,0:T(2,128)(2,1)S(1)} %collective-permute-done.3), channel_id=1, source_target_pairs={{0,1},{1,2},{2,3},{3,4},{4,5},{5,6},{6,7},{7,8},{8,9},{9,10},{10,1... | collective-permute-start | bytes 294920 | tf_op jit(solution)/shard_map/ppermute | solution.py:113
  42.9 17.7 %collective-permute-start.12 = (bf16[8,2,3072]{2,1,0:T(2,128)(2,1)S(1)}, bf16[8,2,3072]{2,1,0:T(2,128)(2,1)}, u32[]{:S(2)}, u32[]{:S(2)}) collective-permute-start(bf16[8,2,3072]{2,1,0:T(2,128)(2,1)S(1)} %collective-permute-done.11), channel_id=1, source_target_pairs={{0,15},{1,0},{2,1},{3,2},{4,3},{5,4},{6,5},{7,6},{8,7},{9,8},{10,9... | collective-permute-start | bytes 294920 | tf_op jit(solution)/shard_map/ppermute | solution.py:115
  50.8 15.2 %collective-permute-start.5 = (bf16[8,2,3072]{2,1,0:T(2,128)(2,1)S(1)}, bf16[8,2,3072]{2,1,0:T(2,128)(2,1)}, u32[]{:S(2)}, u32[]{:S(2)}) collective-permute-start(bf16[8,2,3072]{2,1,0:T(2,128)(2,1)S(1)} %collective-permute-done.4), channel_id=1, source_target_pairs={{0,1},{1,2},{2,3},{3,4},{4,5},{5,6},{6,7},{7,8},{8,9},{9,10},{10,1... | collective-permute-start | bytes 294920 | tf_op jit(solution)/shard_map/ppermute | solution.py:113
  60.6 9.0 %collective-permute-start.13 = (bf16[8,2,3072]{2,1,0:T(2,128)(2,1)}, bf16[8,2,3072]{2,1,0:T(2,128)(2,1)}, u32[]{:S(2)}, u32[]{:S(2)}) collective-permute-start(bf16[8,2,3072]{2,1,0:T(2,128)(2,1)} %collective-permute-done.12), channel_id=1, source_target_pairs={{0,15},{1,0},{2,1},{3,2},{4,3},{5,4},{6,5},{7,6},{8,7},{9,8},{10,9... | collective-permute-start | bytes 294920 | tf_op jit(solution)/shard_map/ppermute | solution.py:115
  66.0 8.9 %collective-permute-start.6 = (bf16[8,2,3072]{2,1,0:T(2,128)(2,1)}, bf16[8,2,3072]{2,1,0:T(2,128)(2,1)}, u32[]{:S(2)}, u32[]{:S(2)}) collective-permute-start(bf16[8,2,3072]{2,1,0:T(2,128)(2,1)} %collective-permute-done.5), channel_id=1, source_target_pairs={{0,1},{1,2},{2,3},{3,4},{4,5},{5,6},{6,7},{7,8},{8,9},{9,10},{10,1... | collective-permute-start | bytes 294920 | tf_op jit(solution)/shard_map/ppermute | solution.py:113
  69.6 7.9 %collective-permute-start.14 = (bf16[8,2,3072]{2,1,0:T(2,128)(2,1)}, bf16[8,2,3072]{2,1,0:T(2,128)(2,1)S(1)}, u32[]{:S(2)}, u32[]{:S(2)}) collective-permute-start(bf16[8,2,3072]{2,1,0:T(2,128)(2,1)} %collective-permute-done.13), channel_id=1, source_target_pairs={{0,15},{1,0},{2,1},{3,2},{4,3},{5,4},{6,5},{7,6},{8,7},{9,8},{10,9... | collective-permute-start | bytes 294920 | tf_op jit(solution)/shard_map/ppermute | solution.py:115
  74.9 8.1 %collective-permute-start.7 = (bf16[8,2,3072]{2,1,0:T(2,128)(2,1)}, bf16[8,2,3072]{2,1,0:T(2,128)(2,1)S(1)}, u32[]{:S(2)}, u32[]{:S(2)}) collective-permute-start(bf16[8,2,3072]{2,1,0:T(2,128)(2,1)} %collective-permute-done.6), channel_id=1, source_target_pairs={{0,1},{1,2},{2,3},{3,4},{4,5},{5,6},{6,7},{7,8},{8,9},{9,10},{10,1... | collective-permute-start | bytes 294920 | tf_op jit(solution)/shard_map/ppermute | solution.py:113
  149.9 81.2 %all-gather.9.cloned.1.call-start = ((), (), s32[]{:S(2)}) async-start(), calls=%async_computation.5 | async-start | bytes 3342336 | tf_op jit(solution)/shard_map/all_gather | solution.py:173
  151.6 172.9 %reduce-scatter.4.cloned.1.call-start = ((), (), s32[]{:S(2)}) async-start(), calls=%async_computation.6 | async-start | bytes 6684672 | tf_op jit(solution)/shard_map/reduce_scatter | solution.py:202
  238.9 85.6 %copy-start.7 = (bf16[8,2,2,3072]{3,2,1,0:T(2,128)(2,1)S(1)}, bf16[8,2,2,3072]{3,2,1,0:T(2,128)(2,1)}, u32[]{:S(2)}) copy-start(bf16[8,2,2,3072]{3,2,1,0:T(2,128)(2,1)} %param.18) | copy-start | bytes 589828
  238.9 85.6 %copy-start.9 = (f32[8,3072]{1,0:T(8,128)S(1)}, f32[8,3072]{1,0:T(8,128)}, u32[]{:S(2)}) copy-start(f32[8,3072]{1,0:T(8,128)} %get-tuple-element.31) | copy-start | bytes 294916
  239.0 140.8 %all-gather.11.cloned.1.call-start = ((), (), s32[]{:S(2)}) async-start(), calls=%async_computation.7 | async-start | bytes 3342336 | tf_op jit(solution)/shard_map/all_gather | solution.py:207
  326.8 161.8 %reduce-scatter.6.cloned.1.call-start = ((), (), s32[]{:S(2)}) async-start(), calls=%async_computation.8 | async-start | bytes 6684672 | tf_op jit(solution)/shard_map/reduce_scatter | solution.py:222
  402.9 169.6 %reduce-scatter.8.cloned.1.call-start = ((), (), s32[]{:S(2)}) async-start(), calls=%async_computation.9 | async-start | bytes 3342336 | tf_op jit(solution)/shard_map/reduce_scatter | solution.py:203
  406.3 82.3 %copy-start.10 = (f32[8,3072]{1,0:T(8,128)S(1)}, f32[8,3072]{1,0:T(8,128)}, u32[]{:S(2)}) copy-start(f32[8,3072]{1,0:T(8,128)} %get-tuple-element.28) | copy-start | bytes 294916
  406.3 85.0 %copy-start.11 = (bf16[3072,64]{0,1:T(8,128)(2,1)S(1)}, bf16[3072,64]{0,1:T(8,128)(2,1)}, u32[]{:S(2)}) copy-start(bf16[3072,64]{0,1:T(8,128)(2,1)} %param.35) | copy-start | bytes 1179652
  406.3 85.3 %copy-start.27 = (f32[8,2,128]{2,1,0:T(2,128)S(1)}, f32[8,2,128]{2,1,0:T(2,128)}, u32[]{:S(2)}) copy-start(f32[8,2,128]{2,1,0:T(2,128)} %param.20) | copy-start | bytes 24580
  491.8 83.3 %collective-permute-start.15 = (f32[8,1,128]{2,1,0:T(1,128)S(1)}, f32[8,1,128]{2,1,0:T(1,128)S(1)}, u32[]{:S(2)}, u32[]{:S(2)}) collective-permute-start(f32[8,1,128]{2,1,0:T(1,128)S(1)} %get-tuple-element.38), channel_id=1, source_target_pairs={{0,16},{16,32},{32,48},{48,64},{64,80},{80,96},{96,112},{112,128},... | collective-permute-start | bytes 12296 | tf_op jit(solution)/shard_map/ppermute | solution.py:21
  493.7 81.4 %collective-permute-start.16 = (f32[8,1,128]{2,1,0:T(1,128)S(1)}, f32[8,1,128]{2,1,0:T(1,128)S(1)}, u32[]{:S(2)}, u32[]{:S(2)}) collective-permute-start(f32[8,1,128]{2,1,0:T(1,128)S(1)} %get-tuple-element.39), channel_id=1, source_target_pairs={{16,0},{32,16},{48,32},{64,48},{80,64},{96,80},{112,96},{128,112},... | collective-permute-start | bytes 12296 | tf_op jit(solution)/shard_map/ppermute | solution.py:22
  (25 other events, 282.2 us)
Sparse Core Ops, SparseCore 0:
  11.0 58.1 all-gather.4
  150.0 38.9 all-gather.6
  191.5 39.6 all-gather.8
  239.1 85.4 reduce-scatter.3
  327.4 52.3 all-gather.10
  403.0 85.5 reduce-scatter.5
  492.2 80.2 reduce-scatter.7
